TPU v7x, 256 devices: a whole 4x4x8 slice. The times are simulated.
256 devices in a mesh: blk: 32 (over z, x_lo, core), col: 8 (over x_hi, y).
Axes of the slice: x: 4 (x_hi: 2, x_lo: 2; x = x_hi * 2 + x_lo), y: 4, z: 8, core: 2. Of those that a mesh axis runs over, the one named last changes fastest.
Arguments:
- feat1: bfloat16 [128, 384, 256], P('blk', 'col'), may hold values from -40 to 40
- feat2: bfloat16 [128, 384, 256], P('blk', 'col'), may hold values from -40 to 40
Outputs:
- flow: float32 [2, 128, 384], P(None, 'blk', 'col')
- grad_flow: float32 [2, 128, 384], P(None, 'blk', 'col')
- grad_warped: float32 [128, 384, 256], P('blk', 'col')
All inputs are finite; a program needn't handle non-finite values.
Results may differ from a plain program's by a relative error of at most 0.0075.
Values may be sent and summed in bfloat16 or wider, within the bound.
No kernel may reach another device: no remote copies, remote signals or barrier semaphores. Data moves between devices by JAX's collectives and lax.ppermute only.
A program may use at most 64 MiB of HBM per device.

v0:
```python
import math
import jax
import jax.numpy as jnp
from jax import lax
from jax.sharding import Mesh
from jax.sharding import PartitionSpec as P

ssim_one = 0.01
ssim_two = 0.03
charb_sq = 0.0001
FINE = ("z", "xl", "c", "xh", "y")
BLK = ("z", "xl", "c")
COL = ("xh", "y")
KEY_AXES = ("z", ("xh", "xl"))
QUERY_AXES = ("y", "c")


def with_halo(value, sides, width):
    for axis, dim in sides:
        count, length = (lax.axis_size(axis), value.shape[dim])
        up = [(i, (i + 1) % count) for i in range(count - 1)]
        down = [(j, i) for i, j in up]
        last = lax.slice_in_dim(value, length - width, length, axis=dim)
        first = lax.slice_in_dim(value, 0, width, axis=dim)
        before = lax.ppermute(last, axis, up)
        after = lax.ppermute(first, axis, down)
        value = jnp.concatenate([before, value, after], axis=dim)
    return value


def box_valid(padded):
    rows_out = padded.shape[0] - 2
    cols_out = padded.shape[1] - 2
    total = jnp.zeros((rows_out, cols_out) + padded.shape[2:], padded.dtype)
    for offset_r in range(3):
        for offset_c in range(3):
            total = total + padded[offset_r : offset_r + rows_out, offset_c : offset_c + cols_out]
    return total / 9.0


def ssim_loss(mean_y, var_y, cov_xy, mean_x, var_x):
    top = (2.0 * mean_x * mean_y + ssim_one) * (2.0 * cov_xy + ssim_two)
    bottom = (mean_x * mean_x + mean_y * mean_y + ssim_one) * (var_x + var_y + ssim_two)
    return jnp.sum((1.0 - top / bottom) * 0.5)


def local_terms(xpad, ypad):
    mean_x = box_valid(xpad)
    mean_y = box_valid(ypad)
    var_x = box_valid(xpad * xpad) - mean_x * mean_x
    var_y = box_valid(ypad * ypad) - mean_y * mean_y
    cov_xy = box_valid(xpad * ypad) - mean_x * mean_y
    loss, pull = jax.vjp(
        lambda one, two, three: ssim_loss(one, two, three, mean_x, var_x), mean_y, var_y, cov_xy
    )
    grad_mean, grad_var, grad_cov = pull(jnp.ones_like(loss))
    first = grad_mean - 2.0 * grad_var * mean_y - grad_cov * mean_x
    return (first, grad_var, grad_cov)


def edge_weight(lower, upper):
    return jnp.exp(-jnp.mean(jnp.abs(upper - lower), axis=-1))


def charbonnier(weight, delta):
    return weight * delta / jnp.sqrt(delta * delta + charb_sq)


def absorb(carry, queries, keys, key_y, key_x, scale):
    total_keys = keys.shape[0]
    width = keys.shape[1]
    step = min(total_keys, 2048)
    while total_keys % step != 0:
        step = step - 1
    blocks = total_keys // step

    def visit(state, item):
        top, total, acc, along_y, along_x = state
        key_block, block_y, block_x = item
        score = (
            lax.dot_general(
                queries, key_block, (((1,), (1,)), ((), ())), preferred_element_type=jnp.float32
            )
            * scale
        )
        new_top = jnp.maximum(top, jnp.max(score, axis=1))
        shrink = jnp.exp(top - new_top)
        expo = jnp.exp(score - new_top[:, None])
        total = total * shrink + jnp.sum(expo, axis=1)
        acc = acc * shrink[:, None] + jnp.dot(
            expo.astype(jnp.bfloat16), key_block, preferred_element_type=jnp.float32
        )
        along_y = along_y * shrink + jnp.sum(expo * block_y[None, :], axis=1)
        along_x = along_x * shrink + jnp.sum(expo * block_x[None, :], axis=1)
        return ((new_top, total, acc, along_y, along_x), None)

    items = (
        keys.reshape(blocks, step, width),
        key_y.reshape(blocks, step),
        key_x.reshape(blocks, step),
    )
    carry, unused = lax.scan(visit, carry, items)
    return carry


def body(feat1, feat2):
    rows, cols, width = feat1.shape
    ncol = lax.axis_size(COL)
    full_rows = rows * lax.axis_size(BLK)
    full_cols = cols * ncol
    row_start = lax.axis_index(BLK) * rows
    col_start = lax.axis_index(COL) * cols
    scale = 1.0 / math.sqrt(width)
    tokens = rows * cols
    queries = lax.all_gather(feat1.reshape(tokens, width), QUERY_AXES, axis=0, tiled=True)
    group = queries.shape[0]
    init = (
        jnp.full((group,), -1e30, jnp.float32),
        jnp.zeros((group,), jnp.float32),
        jnp.zeros((group, width), jnp.float32),
        jnp.zeros((group,), jnp.float32),
        jnp.zeros((group,), jnp.float32),
    )

    def norm_y(index):
        return (index.astype(jnp.float32) + 0.5) * (2.0 / full_rows) - 1.0

    def norm_x(index):
        return (index.astype(jnp.float32) + 0.5) * (2.0 / full_cols) - 1.0

    piece = feat2
    for axis in KEY_AXES:
        piece = lax.all_gather(piece, axis, axis=0, tiled=True)
    count = piece.shape[0]
    gathered = jnp.arange(count, dtype=jnp.int32)
    rest = gathered // rows
    place = {}
    for axis in KEY_AXES:
        size = lax.axis_size(axis)
        place[axis] = rest % size
        rest = rest // size
    sz, sxl, sc, sxh, sy = (lax.axis_size(a) for a in FINE)
    x_full = place["xh", "xl"]
    blk_of = (place["z"] * sxl + x_full % sxl) * sc + lax.axis_index("c")
    col_of = x_full // sxl * sy + lax.axis_index("y")
    tile_y = blk_of * rows + gathered % rows
    tile_x = col_of * cols
    grid_y = jnp.broadcast_to(tile_y[:, None], (count, cols))
    grid_x = tile_x[:, None] + jnp.arange(cols, dtype=jnp.int32)[None, :]
    carry = absorb(
        init,
        queries,
        piece.reshape(count * cols, width),
        norm_y(grid_y).reshape(-1),
        norm_x(grid_x).reshape(-1),
        scale,
    )
    top, total, acc, along_y, along_x = carry
    parts = lax.axis_size(QUERY_AXES)
    stats = jnp.stack([top, total, along_y, along_x]).reshape(4, parts, tokens)
    stats = jnp.pad(stats.transpose(1, 0, 2), ((0, 0), (0, 0), (0, width - tokens)))
    packed = jnp.concatenate([acc.reshape(parts, tokens, width), stats], axis=1)
    packed = lax.all_to_all(packed, QUERY_AXES, 0, 0, tiled=True)
    tops = packed[:, tokens, :tokens]
    peak = jnp.max(tops, axis=0)
    factor = jnp.exp(tops - peak[None])
    acc = jnp.sum(packed[:, :tokens, :] * factor[:, :, None], axis=0)
    total = jnp.sum(packed[:, tokens + 1, :tokens] * factor, axis=0)
    along_y = jnp.sum(packed[:, tokens + 2, :tokens] * factor, axis=0)
    along_x = jnp.sum(packed[:, tokens + 3, :tokens] * factor, axis=0)
    warped = (acc / total[:, None]).astype(jnp.bfloat16).reshape(rows, cols, width)
    own_y = norm_y(row_start + jnp.arange(rows, dtype=jnp.int32))
    own_x = norm_x(col_start + jnp.arange(cols, dtype=jnp.int32))
    flow = jnp.stack(
        [
            (along_y / total).reshape(rows, cols) - own_y[:, None],
            (along_x / total).reshape(rows, cols) - own_x[None, :],
        ]
    )
    pair = jnp.stack([feat1, warped])
    xval = feat1.astype(jnp.float32)
    yval = warped.astype(jnp.float32)
    margin = 1
    padded = with_halo(pair, ((BLK, 1), (COL, 2)), 1)
    xpad = padded[0].astype(jnp.float32)
    ypad = padded[1].astype(jnp.float32)
    first, grad_var, grad_cov = local_terms(xpad, ypad)
    maps = jnp.stack([first, grad_var, grad_cov])
    beside_all = with_halo(maps.astype(jnp.bfloat16), ((BLK, 1), (COL, 2)), 1).astype(maps.dtype)
    spread_first = box_valid(beside_all[0])
    spread_var = box_valid(beside_all[1])
    spread_cov = box_valid(beside_all[2])
    grad_warped = spread_first + 2.0 * yval * spread_var + xval * spread_cov
    flow_pad = with_halo(flow, ((BLK, 1), (COL, 2)), 1)
    x_rows = xpad[margin - 1 : margin + rows + 1, margin : margin + cols]
    x_cols = xpad[margin : margin + rows, margin - 1 : margin + cols + 1]
    edge_y = row_start - 1 + jnp.arange(rows + 1, dtype=jnp.int32)
    valid_y = (edge_y >= 0) & (edge_y <= full_rows - 2)
    edge_x = col_start - 1 + jnp.arange(cols + 1, dtype=jnp.int32)
    valid_x = (edge_x >= 0) & (edge_x <= full_cols - 2)
    delta_y = flow_pad[:, 1:, 1:-1] - flow_pad[:, :-1, 1:-1]
    push_y = jnp.where(
        valid_y[None, :, None],
        charbonnier(edge_weight(x_rows[:-1], x_rows[1:])[None], delta_y),
        0.0,
    )
    delta_x = flow_pad[:, 1:-1, 1:] - flow_pad[:, 1:-1, :-1]
    push_x = jnp.where(
        valid_x[None, None, :],
        charbonnier(edge_weight(x_cols[:, :-1], x_cols[:, 1:])[None], delta_x),
        0.0,
    )
    grad_flow = push_y[:, :rows] - push_y[:, 1:] + push_x[:, :, :cols] - push_x[:, :, 1:]
    return (flow, grad_flow, grad_warped)


def solution(mesh):
    blk, col = mesh.devices.shape
    fine = mesh.devices.reshape(blk // 4, 2, 2, 2, col // 2)
    fine_mesh = Mesh(fine, FINE)
    placed = (P(BLK, COL, None), P(BLK, COL, None))
    return jax.shard_map(
        body,
        mesh=fine_mesh,
        in_specs=placed,
        out_specs=(P(None, BLK, COL), P(None, BLK, COL), P(BLK, COL, None)),
        check_vma=False,
    )
```

profile of v0, /device:TPU:132, one launch (start us, length us, event | category | flops | bytes accessed | tf_op | source)
XLA Modules:
  0.0 233.7 jit_solution(6486698609514709676)
XLA Ops:
  7.2 28.3 %all_gather.9 = bf16[32,48,256]{2,1,0:T(8,128)(2,1)} all-gather(bf16[4,48,256]{2,1,0:T(8,128)(2,1)} %param.5), channel_id=1, replica_groups=mesh['z'=8,'xl'=2,'c'=2,'xh'=2,'y'=4] {'z'}, dimensions={0}, use_global_device_ids=true | all-gather | bytes 884736 | tf_op jit(solution)/shard_map/all_gather | solution.py:133
  36.0 14.1 %all_gather.11 = bf16[1536,256]{1,0:T(8,128)(2,1)S(1)} all-gather(bf16[192,256]{1,0:T(8,128)(2,1)} %bitcast.82), channel_id=1, replica_groups=mesh['z'=8,'xl'=2,'c'=2,'xh'=2,'y'=4] {'y','c'}, dimensions={0}, use_global_device_ids=true | all-gather | bytes 884736 | tf_op jit(solution)/shard_map/all_gather | solution.py:115
  50.2 27.9 %all-gather.2.cloned.1.call-done = bf16[128,48,256]{2,1,0:T(8,128)(2,1)} async-done(((bf16[32,48,256]{2,1,0:T(8,128)(2,1)}), bf16[128,48,256]{2,1,0:T(8,128)(2,1)}) %all-gather.2.cloned.1.call-update) | async-done | bytes 3145744 | tf_op jit(solution)/shard_map/all_gather | solution.py:133
  78.1 60.4 %while.19 = (s32[]{:T(128)}, f32[1536]{0:T(1024)S(1)}, f32[1536]{0:T(1024)S(1)}, f32[1536,256]{1,0:T(8,128)S(1)}, f32[1536]{0:T(1024)S(1)}, /*index=5*/f32[1536]...) while((s32[]{:T(128)}, f32[1536]{0:T(1024)S(1)}, ...), condition=%wide.region_5.6_spmd.clone, body=%wide.region_0.5_spmd.clone.sunk | while | flops 3260167680 | bytes 94312616 | solution.py:102
  78.1 7.6 %multiply_reduce_fusion.5 = (f32[1536]{0:T(1024)S(1)}, f32[2048,1536]{1,0:T(8,128)}) fusion(bf16[1536,256]{1,0:T(8,128)(2,1)S(1)} %get-tuple-element.282, bf16[3,2048,256]{2,1,0:T(8,128)(2,1)} %get-tuple-element.281, s32[]{:T(128)S(6)} %copy.42), kind=kOutput, calls=%fused_computation.3.clone.1 | convolution fusion | flops 1616902656 | bytes 14424068 | tf_op jit(solution)/shard_map/while/body/eval_jaxpr/dot_general | solution.py:81
  85.7 8.5 %multiply_reduce_fusion.6 = (f32[1536]{0:T(1024)S(1)}, f32[1536]{0:T(1024)S(1)}, f32[1536]{0:T(1024)S(1)}) fusion(f32[2048]{0:T(1024)S(1)} %bitcast.89, f32[1536]{0:T(1024)S(1)} %select_maximum_fusion.3, f32[2048,1536]{1,0:T(8,128)} %get-tuple-element.242, f32[2048]{0:T(1024)S(1)} %bitcast.90), kind=kLoop, calls=%fused_computation.clone.1 | loop fusion | flops 22015488 | bytes 12623872 | tf_op jit(solution)/shard_map/while/body/eval_jaxpr/reduce_sum | solution.py:94
  94.3 3.9 %fusion.89 = f32[1536,256]{1,0:T(8,128)S(1)} fusion(f32[1536]{0:T(1024)S(1)} %select_maximum_fusion.3, f32[2048,1536]{1,0:T(8,128)S(1)} %copy-done, f32[1536,256]{1,0:T(8,128)S(1)} %get-tuple-element.266, bf16[3,2048,256]{2,1,0:T(8,128)(2,1)} %get-tuple-element.281, s32[]{:T(128)S(6)} %copy.42, f32[1536]{0:T(1024)S(1)} %get-tuple-element.246, ...), kind=kOutput, calls=%fused_computation.7.clone.1 | convolution fusion | flops 1621229568 | bytes 16789508 | tf_op jit(solution)/shard_map/while/body/eval_jaxpr/dot_general | solution.py:90
  98.3 7.6 %multiply_reduce_fusion.5 = (f32[1536]{0:T(1024)S(1)}, f32[2048,1536]{1,0:T(8,128)}) fusion(bf16[1536,256]{1,0:T(8,128)(2,1)S(1)} %get-tuple-element.282, bf16[3,2048,256]{2,1,0:T(8,128)(2,1)} %get-tuple-element.281, s32[]{:T(128)S(6)} %copy.42), kind=kOutput, calls=%fused_computation.3.clone.1 | convolution fusion | flops 1616902656 | bytes 14424068 | tf_op jit(solution)/shard_map/while/body/eval_jaxpr/dot_general | solution.py:81
  105.9 8.5 %multiply_reduce_fusion.6 = (f32[1536]{0:T(1024)S(1)}, f32[1536]{0:T(1024)S(1)}, f32[1536]{0:T(1024)S(1)}) fusion(f32[2048]{0:T(1024)S(1)} %bitcast.89, f32[1536]{0:T(1024)S(1)} %select_maximum_fusion.3, f32[2048,1536]{1,0:T(8,128)} %get-tuple-element.242, f32[2048]{0:T(1024)S(1)} %bitcast.90), kind=kLoop, calls=%fused_computation.clone.1 | loop fusion | flops 22015488 | bytes 12623872 | tf_op jit(solution)/shard_map/while/body/eval_jaxpr/reduce_sum | solution.py:94
  114.4 3.9 %fusion.89 = f32[1536,256]{1,0:T(8,128)S(1)} fusion(f32[1536]{0:T(1024)S(1)} %select_maximum_fusion.3, f32[2048,1536]{1,0:T(8,128)S(1)} %copy-done, f32[1536,256]{1,0:T(8,128)S(1)} %get-tuple-element.266, bf16[3,2048,256]{2,1,0:T(8,128)(2,1)} %get-tuple-element.281, s32[]{:T(128)S(6)} %copy.42, f32[1536]{0:T(1024)S(1)} %get-tuple-element.246, ...), kind=kOutput, calls=%fused_computation.7.clone.1 | convolution fusion | flops 1621229568 | bytes 16789508 | tf_op jit(solution)/shard_map/while/body/eval_jaxpr/dot_general | solution.py:90
  118.4 7.6 %multiply_reduce_fusion.5 = (f32[1536]{0:T(1024)S(1)}, f32[2048,1536]{1,0:T(8,128)}) fusion(bf16[1536,256]{1,0:T(8,128)(2,1)S(1)} %get-tuple-element.282, bf16[3,2048,256]{2,1,0:T(8,128)(2,1)} %get-tuple-element.281, s32[]{:T(128)S(6)} %copy.42), kind=kOutput, calls=%fused_computation.3.clone.1 | convolution fusion | flops 1616902656 | bytes 14424068 | tf_op jit(solution)/shard_map/while/body/eval_jaxpr/dot_general | solution.py:81
  126.0 8.5 %multiply_reduce_fusion.6 = (f32[1536]{0:T(1024)S(1)}, f32[1536]{0:T(1024)S(1)}, f32[1536]{0:T(1024)S(1)}) fusion(f32[2048]{0:T(1024)S(1)} %bitcast.89, f32[1536]{0:T(1024)S(1)} %select_maximum_fusion.3, f32[2048,1536]{1,0:T(8,128)} %get-tuple-element.242, f32[2048]{0:T(1024)S(1)} %bitcast.90), kind=kLoop, calls=%fused_computation.clone.1 | loop fusion | flops 22015488 | bytes 12623872 | tf_op jit(solution)/shard_map/while/body/eval_jaxpr/reduce_sum | solution.py:94
  134.6 3.9 %fusion.89 = f32[1536,256]{1,0:T(8,128)S(1)} fusion(f32[1536]{0:T(1024)S(1)} %select_maximum_fusion.3, f32[2048,1536]{1,0:T(8,128)S(1)} %copy-done, f32[1536,256]{1,0:T(8,128)S(1)} %get-tuple-element.266, bf16[3,2048,256]{2,1,0:T(8,128)(2,1)} %get-tuple-element.281, s32[]{:T(128)S(6)} %copy.42, f32[1536]{0:T(1024)S(1)} %get-tuple-element.246, ...), kind=kOutput, calls=%fused_computation.7.clone.1 | convolution fusion | flops 1621229568 | bytes 16789508 | tf_op jit(solution)/shard_map/while/body/eval_jaxpr/dot_general | solution.py:90
  138.9 1.3 select_maximum_fusion.1
  140.2 4.4 %all-to-all-start = ((f32[8,196,256]{2,1,0:T(8,128)}), f32[8,196,256]{2,1,0:T(8,128)S(1)}, u32[]{:S(2)}, u32[]{:S(2)}) async-start(f32[8,196,256]{2,1,0:T(8,128)} %select_maximum_fusion.1), calls=%async_computation | async-start | bytes 3276800 | tf_op jit(solution)/shard_map/all_to_all | solution.py:163
  144.7 22.2 %all-to-all-done = f32[8,196,256]{2,1,0:T(8,128)S(1)} async-done(((f32[8,196,256]{2,1,0:T(8,128)}), f32[8,196,256]{2,1,0:T(8,128)S(1)}, u32[]{:S(2)}, u32[]{:S(2)}) %all-to-all-start) | async-done | bytes 1605664 | tf_op jit(solution)/shard_map/all_to_all | solution.py:163
  167.3 1.9 collective-permute-start.4
  169.3 2.4 %collective-permute-start.5 = (f32[2,1,48]{2,1,0:T(1,128)S(1)}, f32[2,1,48]{2,1,0:T(1,128)S(1)}, u32[]{:S(2)}, u32[]{:S(2)}) collective-permute-start(f32[2,1,48]{2,1,0:T(1,128)S(1)} %get-tuple-element.162), channel_id=1, source_target_pairs={{0,8},{8,16},{16,24},{24,32},{32,40},{40,48},{48,56},{56,64},{64,7... | collective-permute-start | bytes 1160 | tf_op jit(solution)/shard_map/ppermute | solution.py:25
  172.7 5.3 %collective-permute-start.1 = (bf16[2,1,48,256]{3,2,1,0:T(8,128)(2,1)S(1)}, bf16[2,1,48,256]{3,2,1,0:T(8,128)(2,1)S(1)}, u32[]{:S(2)}, u32[]{:S(2)}) collective-permute-start(bf16[2,1,48,256]{3,2,1,0:T(8,128)(2,1)S(1)} %get-tuple-element.159), channel_id=1, source_target_pairs={{8,0},{16,8},{24,16},{32,24},{40,32},{48,40},{56,48},{64,56},{72,6... | collective-permute-start | bytes 147464 | tf_op jit(solution)/shard_map/ppermute | solution.py:26
  177.9 1.9 collective-permute-start
  179.9 5.5 %collective-permute-done = bf16[2,1,48,256]{3,2,1,0:T(8,128)(2,1)S(1)} collective-permute-done((bf16[2,1,48,256]{3,2,1,0:T(8,128)(2,1)S(1)}, bf16[2,1,48,256]{3,2,1,0:T(8,128)(2,1)S(1)}, u32[]{:S(2)}, u32[]{:S(2)}) %collective-permute-start) | collective-permute-done | bytes 49184 | tf_op jit(solution)/shard_map/ppermute | solution.py:25
  185.5 4.1 %collective-permute-start.3 = (bf16[2,6,1,256]{3,2,1,0:T(2,128)(2,1)S(1)}, bf16[2,6,1,256]{3,2,1,0:T(2,128)(2,1)S(1)}, u32[]{:S(2)}, u32[]{:S(2)}) collective-permute-start(bf16[2,6,1,256]{3,2,1,0:T(2,128)(2,1)S(1)} %get-tuple-element.157), channel_id=1, source_target_pairs={{1,0},{2,1},{3,2},{4,3},{5,4},{6,5},{7,6},{9,8},{10,9},{11,10},{12... | collective-permute-start | bytes 18440 | tf_op jit(solution)/shard_map/ppermute | solution.py:26
  189.6 1.9 collective-permute-start.2
  191.6 2.3 collective-permute-start.7
  193.9 7.2 %collective-permute-start.6 = (f32[2,6,1]{2,1,0:T(8,128)S(1)}, f32[2,6,1]{2,1,0:T(8,128)S(1)}, u32[]{:S(2)}, u32[]{:S(2)}) collective-permute-start(f32[2,6,1]{2,1,0:T(8,128)S(1)} %get-tuple-element.160), channel_id=1, source_target_pairs={{1,0},{2,1},{3,2},{4,3},{5,4},{6,5},{7,6},{9,8},{10,9},{11,10},{12... | collective-permute-start | bytes 152 | tf_op jit(solution)/shard_map/ppermute | solution.py:26
  202.6 1.9 collective-permute-start.9
  204.5 2.4 %collective-permute-start.8 = (bf16[3,1,48,256]{3,2,1,0:T(8,128)(2,1)S(1)}, bf16[3,1,48,256]{3,2,1,0:T(8,128)(2,1)S(1)}, u32[]{:S(2)}, u32[]{:S(2)}) collective-permute-start(bf16[3,1,48,256]{3,2,1,0:T(8,128)(2,1)S(1)} %get-tuple-element.154), channel_id=1, source_target_pairs={{0,8},{8,16},{16,24},{24,32},{32,40},{40,48},{48,56},{56,64},{64,7... | collective-permute-start | bytes 221192 | tf_op jit(solution)/shard_map/ppermute | solution.py:25
  207.1 5.2 %collective-permute-done.8 = bf16[3,1,48,256]{3,2,1,0:T(8,128)(2,1)S(1)} collective-permute-done((bf16[3,1,48,256]{3,2,1,0:T(8,128)(2,1)S(1)}, bf16[3,1,48,256]{3,2,1,0:T(8,128)(2,1)S(1)}, u32[]{:S(2)}, u32[]{:S(2)}) %collective-permute-start.8) | collective-permute-done | bytes 73760 | tf_op jit(solution)/shard_map/ppermute | solution.py:25
  212.4 3.9 %collective-permute-start.11 = (bf16[3,6,1,256]{3,2,1,0:T(2,128)(2,1)S(1)}, bf16[3,6,1,256]{3,2,1,0:T(2,128)(2,1)S(1)}, u32[]{:S(2)}, u32[]{:S(2)}) collective-permute-start(bf16[3,6,1,256]{3,2,1,0:T(2,128)(2,1)S(1)} %get-tuple-element.148), channel_id=1, source_target_pairs={{1,0},{2,1},{3,2},{4,3},{5,4},{6,5},{7,6},{9,8},{10,9},{11,10},{12... | collective-permute-start | bytes 27656 | tf_op jit(solution)/shard_map/ppermute | solution.py:26
  216.3 1.9 collective-permute-start.10
  218.9 6.7 %collective-permute-done.10 = bf16[3,6,1,256]{3,2,1,0:T(2,128)(2,1)S(1)} collective-permute-done((bf16[3,6,1,256]{3,2,1,0:T(2,128)(2,1)S(1)}, bf16[3,6,1,256]{3,2,1,0:T(2,128)(2,1)S(1)}, u32[]{:S(2)}, u32[]{:S(2)}) %collective-permute-start.10) | collective-permute-done | bytes 9248 | tf_op jit(solution)/shard_map/ppermute | solution.py:25
  225.8 1.0 fusion.24
  (85 shorter events, 5.1 us)
Async XLA Ops:
  7.2 70.9 %all-gather.2.cloned.1.call-start = ((), (), s32[]{:S(2)}) async-start(), calls=%async_computation.1 | async-start | bytes 3932160 | tf_op jit(solution)/shard_map/all_gather | solution.py:133
  85.7 8.5 %copy-start = (f32[2048,1536]{1,0:T(8,128)S(1)}, f32[2048,1536]{1,0:T(8,128)}, u32[]{:S(2)}) copy-start(f32[2048,1536]{1,0:T(8,128)} %get-tuple-element.242) | copy-start | bytes 37748740 | tf_op jit(solution)/shard_map/while
  105.9 8.5 %copy-start = (f32[2048,1536]{1,0:T(8,128)S(1)}, f32[2048,1536]{1,0:T(8,128)}, u32[]{:S(2)}) copy-start(f32[2048,1536]{1,0:T(8,128)} %get-tuple-element.242) | copy-start | bytes 37748740 | tf_op jit(solution)/shard_map/while
  126.0 8.5 %copy-start = (f32[2048,1536]{1,0:T(8,128)S(1)}, f32[2048,1536]{1,0:T(8,128)}, u32[]{:S(2)}) copy-start(f32[2048,1536]{1,0:T(8,128)} %get-tuple-element.242) | copy-start | bytes 37748740 | tf_op jit(solution)/shard_map/while
  140.2 31.8 %copy-start.1 = (bf16[4,48,256]{2,1,0:T(8,128)(2,1)S(1)}, bf16[4,48,256]{2,1,0:T(8,128)(2,1)}, u32[]{:S(2)}) copy-start(bf16[4,48,256]{2,1,0:T(8,128)(2,1)} %param.4) | copy-start | bytes 294916
  140.2 26.7 %all-to-all-start = ((f32[8,196,256]{2,1,0:T(8,128)}), f32[8,196,256]{2,1,0:T(8,128)S(1)}, u32[]{:S(2)}, u32[]{:S(2)}) async-start(f32[8,196,256]{2,1,0:T(8,128)} %select_maximum_fusion.1), calls=%async_computation | async-start | bytes 3276800 | tf_op jit(solution)/shard_map/all_to_all | solution.py:163
  167.3 12.5 %collective-permute-start.4 = (f32[2,1,48]{2,1,0:T(1,128)S(1)}, f32[2,1,48]{2,1,0:T(1,128)S(1)}, u32[]{:S(2)}, u32[]{:S(2)}) collective-permute-start(f32[2,1,48]{2,1,0:T(1,128)S(1)} %get-tuple-element.163), channel_id=1, source_target_pairs={{8,0},{16,8},{24,16},{32,24},{40,32},{48,40},{56,48},{64,56},{72,6... | collective-permute-start | bytes 1160 | tf_op jit(solution)/shard_map/ppermute | solution.py:26
  169.3 10.6 %collective-permute-start.5 = (f32[2,1,48]{2,1,0:T(1,128)S(1)}, f32[2,1,48]{2,1,0:T(1,128)S(1)}, u32[]{:S(2)}, u32[]{:S(2)}) collective-permute-start(f32[2,1,48]{2,1,0:T(1,128)S(1)} %get-tuple-element.162), channel_id=1, source_target_pairs={{0,8},{8,16},{16,24},{24,32},{32,40},{40,48},{48,56},{56,64},{64,7... | collective-permute-start | bytes 1160 | tf_op jit(solution)/shard_map/ppermute | solution.py:25
  172.7 7.2 %collective-permute-start.1 = (bf16[2,1,48,256]{3,2,1,0:T(8,128)(2,1)S(1)}, bf16[2,1,48,256]{3,2,1,0:T(8,128)(2,1)S(1)}, u32[]{:S(2)}, u32[]{:S(2)}) collective-permute-start(bf16[2,1,48,256]{3,2,1,0:T(8,128)(2,1)S(1)} %get-tuple-element.159), channel_id=1, source_target_pairs={{8,0},{16,8},{24,16},{32,24},{40,32},{48,40},{56,48},{64,56},{72,6... | collective-permute-start | bytes 147464 | tf_op jit(solution)/shard_map/ppermute | solution.py:26
  177.9 7.5 %collective-permute-start = (bf16[2,1,48,256]{3,2,1,0:T(8,128)(2,1)S(1)}, bf16[2,1,48,256]{3,2,1,0:T(8,128)(2,1)S(1)}, u32[]{:S(2)}, u32[]{:S(2)}) collective-permute-start(bf16[2,1,48,256]{3,2,1,0:T(8,128)(2,1)S(1)} %get-tuple-element.158), channel_id=1, source_target_pairs={{0,8},{8,16},{16,24},{24,32},{32,40},{40,48},{48,56},{56,64},{64,7... | collective-permute-start | bytes 147464 | tf_op jit(solution)/shard_map/ppermute | solution.py:25
  185.5 15.6 %collective-permute-start.3 = (bf16[2,6,1,256]{3,2,1,0:T(2,128)(2,1)S(1)}, bf16[2,6,1,256]{3,2,1,0:T(2,128)(2,1)S(1)}, u32[]{:S(2)}, u32[]{:S(2)}) collective-permute-start(bf16[2,6,1,256]{3,2,1,0:T(2,128)(2,1)S(1)} %get-tuple-element.157), channel_id=1, source_target_pairs={{1,0},{2,1},{3,2},{4,3},{5,4},{6,5},{7,6},{9,8},{10,9},{11,10},{12... | collective-permute-start | bytes 18440 | tf_op jit(solution)/shard_map/ppermute | solution.py:26
  189.6 11.5 %collective-permute-start.2 = (bf16[2,6,1,256]{3,2,1,0:T(2,128)(2,1)S(1)}, bf16[2,6,1,256]{3,2,1,0:T(2,128)(2,1)S(1)}, u32[]{:S(2)}, u32[]{:S(2)}) collective-permute-start(bf16[2,6,1,256]{3,2,1,0:T(2,128)(2,1)S(1)} %get-tuple-element.156), channel_id=1, source_target_pairs={{0,1},{1,2},{2,3},{3,4},{4,5},{5,6},{6,7},{8,9},{9,10},{10,11},{11... | collective-permute-start | bytes 18440 | tf_op jit(solution)/shard_map/ppermute | solution.py:25
  191.6 15.4 %collective-permute-start.7 = (f32[2,6,1]{2,1,0:T(8,128)S(1)}, f32[2,6,1]{2,1,0:T(8,128)S(1)}, u32[]{:S(2)}, u32[]{:S(2)}) collective-permute-start(f32[2,6,1]{2,1,0:T(8,128)S(1)} %get-tuple-element.161), channel_id=1, source_target_pairs={{0,1},{1,2},{2,3},{3,4},{4,5},{5,6},{6,7},{8,9},{9,10},{10,11},{11... | collective-permute-start | bytes 152 | tf_op jit(solution)/shard_map/ppermute | solution.py:25
  193.9 13.1 %collective-permute-start.6 = (f32[2,6,1]{2,1,0:T(8,128)S(1)}, f32[2,6,1]{2,1,0:T(8,128)S(1)}, u32[]{:S(2)}, u32[]{:S(2)}) collective-permute-start(f32[2,6,1]{2,1,0:T(8,128)S(1)} %get-tuple-element.160), channel_id=1, source_target_pairs={{1,0},{2,1},{3,2},{4,3},{5,4},{6,5},{7,6},{9,8},{10,9},{11,10},{12... | collective-permute-start | bytes 152 | tf_op jit(solution)/shard_map/ppermute | solution.py:26
  202.6 4.5 %collective-permute-start.9 = (bf16[3,1,48,256]{3,2,1,0:T(8,128)(2,1)S(1)}, bf16[3,1,48,256]{3,2,1,0:T(8,128)(2,1)S(1)}, u32[]{:S(2)}, u32[]{:S(2)}) collective-permute-start(bf16[3,1,48,256]{3,2,1,0:T(8,128)(2,1)S(1)} %get-tuple-element.155), channel_id=1, source_target_pairs={{8,0},{16,8},{24,16},{32,24},{40,32},{48,40},{56,48},{64,56},{72,6... | collective-permute-start | bytes 221192 | tf_op jit(solution)/shard_map/ppermute | solution.py:26
  204.5 7.8 %collective-permute-start.8 = (bf16[3,1,48,256]{3,2,1,0:T(8,128)(2,1)S(1)}, bf16[3,1,48,256]{3,2,1,0:T(8,128)(2,1)S(1)}, u32[]{:S(2)}, u32[]{:S(2)}) collective-permute-start(bf16[3,1,48,256]{3,2,1,0:T(8,128)(2,1)S(1)} %get-tuple-element.154), channel_id=1, source_target_pairs={{0,8},{8,16},{16,24},{24,32},{32,40},{40,48},{48,56},{56,64},{64,7... | collective-permute-start | bytes 221192 | tf_op jit(solution)/shard_map/ppermute | solution.py:25
  212.4 6.5 %collective-permute-start.11 = (bf16[3,6,1,256]{3,2,1,0:T(2,128)(2,1)S(1)}, bf16[3,6,1,256]{3,2,1,0:T(2,128)(2,1)S(1)}, u32[]{:S(2)}, u32[]{:S(2)}) collective-permute-start(bf16[3,6,1,256]{3,2,1,0:T(2,128)(2,1)S(1)} %get-tuple-element.148), channel_id=1, source_target_pairs={{1,0},{2,1},{3,2},{4,3},{5,4},{6,5},{7,6},{9,8},{10,9},{11,10},{12... | collective-permute-start | bytes 27656 | tf_op jit(solution)/shard_map/ppermute | solution.py:26
  216.3 9.3 %collective-permute-start.10 = (bf16[3,6,1,256]{3,2,1,0:T(2,128)(2,1)S(1)}, bf16[3,6,1,256]{3,2,1,0:T(2,128)(2,1)S(1)}, u32[]{:S(2)}, u32[]{:S(2)}) collective-permute-start(bf16[3,6,1,256]{3,2,1,0:T(2,128)(2,1)S(1)} %get-tuple-element.147), channel_id=1, source_target_pairs={{0,1},{1,2},{2,3},{3,4},{4,5},{5,6},{6,7},{8,9},{9,10},{10,11},{11... | collective-permute-start | bytes 27656 | tf_op jit(solution)/shard_map/ppermute | solution.py:25
Sparse Core Ops, SparseCore 0:
  35.6 42.4 all-gather.1
where the time goes:
time: 234 us
  waiting for transfers between devices  67.6 us (29%)
  blocking collectives  42.4 us (18%)
  starting transfers between devices  41.6 us (18%)
  matrix products  34.6 us (15%)
  other arithmetic  31.7 us (14%)
  between operations  14.4 us (6%)
    all_gather x1, blocking collectives, body(): piece = lax.all_gather(piece, axis, axis=0, tiled=True)  28.3 us
    all_gather x1, waiting for transfers between devices, body(): piece = lax.all_gather(piece, axis, axis=0, tiled=True)  27.9 us
    reduce_sum x3, other arithmetic, visit(): along_x = along_x * shrink + jnp.sum(expo * block_x[None, :], axis=1)  25.5 us
    ppermute x6, starting transfers between devices, with_halo(): after = lax.ppermute(first, axis, down)  24.3 us
    dot_general x3, matrix products, visit(): lax.dot_general(queries, key_block, (((1,), (1,)), ((), ())), preferred_e...  22.8 us
    all_to_all x1, waiting for transfers between devices, body(): packed = lax.all_to_all(packed, QUERY_AXES, 0, 0, tiled=True)  22.2 us
    ppermute x6, waiting for transfers between devices, with_halo(): before = lax.ppermute(last, axis, up)  17.4 us
    all_gather x1, blocking collectives, body(): lax.all_gather(feat1.reshape(tokens, width), QUERY_AXES, axis=0, tiled=True)  14.1 us
  transfers between devices with their start and end apart: 14, of which 5 were waited for; matrix products, arithmetic and copies ran while one was open for 2% of the time, Pallas kernels for 0%

commit v1 on v0

--- a/solution.py
+++ b/solution.py
@@ -112,7 +112,12 @@
     col_start = lax.axis_index(COL) * cols
     scale = 1.0 / math.sqrt(width)
     tokens = rows * cols
-    queries = lax.all_gather(feat1.reshape(tokens, width), QUERY_AXES, axis=0, tiled=True)
+    queries = jnp.concatenate(
+        lax.all_to_all(
+            jnp.stack([feat1.reshape(tokens, width)] * lax.axis_size(QUERY_AXES)), QUERY_AXES, 0, 0
+        ),
+        axis=0,
+    )
     group = queries.shape[0]
     init = (
         jnp.full((group,), -1e30, jnp.float32),

time: 234 us -> 234 us (level)
  blocking collectives: 42.4 us -> 28.3 us
  waiting for transfers between devices: 67.6 us -> 75.4 us
  starting transfers between devices: 41.6 us -> 46.1 us
    all_gather x1 -> x0, blocking collectives: 14.1 us -> none  [body(): lax.all_gather(feat1.reshape(tokens, width), QUERY_AXES, axis=0, tiled=True)]
    all_to_all x0 -> x1, waiting for transfers between devices: none -> 12.6 us  [body(): lax.all_to_all(jnp.stack([feat1.reshape(tokens, width)] * lax.axis_size(Q...]
    all_gather x1, waiting for transfers between devices: 27.9 us -> 23.1 us  [body(): piece = lax.all_gather(piece, axis, axis=0, tiled=True)]
    all_to_all x0 -> x1, starting transfers between devices: none -> 4.47 us  [body(): lax.all_to_all(jnp.stack([feat1.reshape(tokens, width)] * lax.axis_size(Q...]
  transfers between devices with their start and end apart: 14 -> 15, of which waited for: 5 -> 6; matrix products, arithmetic and copies ran while one was open for 2% -> 2% of each run, Pallas kernels for 0% -> 0%
where the time goes in v1:
time: 234 us; the launch traced here: 233 us
  waiting for transfers between devices  75.4 us (32%)
  starting transfers between devices  46.1 us (20%)
  matrix products  34.6 us (15%)
  other arithmetic  31.6 us (14%)
  blocking collectives  28.3 us (12%)
  between operations  14.4 us (6%)
  local copies, waits for them, and re-layouts  2.94 us (1%)
    all_gather x1, blocking collectives, body(): piece = lax.all_gather(piece, axis, axis=0, tiled=True)  28.3 us
    reduce_sum x3, other arithmetic, visit(): along_x = along_x * shrink + jnp.sum(expo * block_x[None, :], axis=1)  25.3 us
    ppermute x6, starting transfers between devices, with_halo(): after = lax.ppermute(first, axis, down)  24.3 us
    all_gather x1, waiting for transfers between devices, body(): piece = lax.all_gather(piece, axis, axis=0, tiled=True)  23.1 us
    dot_general x3, matrix products, visit(): lax.dot_general(queries, key_block, (((1,), (1,)), ((), ())), preferred_e...  22.8 us
    all_to_all x1, waiting for transfers between devices, body(): packed = lax.all_to_all(packed, QUERY_AXES, 0, 0, tiled=True)  22.2 us
    ppermute x6, waiting for transfers between devices, with_halo(): before = lax.ppermute(last, axis, up)  17.4 us
    ppermute x6, starting transfers between devices, with_halo(): before = lax.ppermute(last, axis, up)  12.8 us
  transfers between devices with their start and end apart: 15, of which 6 were waited for; matrix products, arithmetic and copies ran while one was open for 2% of the time, Pallas kernels for 0%

profile of v1, /device:TPU:132, one launch (start us, length us, event | category | flops | bytes accessed | tf_op | source)
XLA Modules:
  0.0 233.5 jit_solution(8043925656016477180)
XLA Ops:
  7.2 28.3 %all_gather.6 = bf16[32,48,256]{2,1,0:T(8,128)(2,1)} all-gather(bf16[4,48,256]{2,1,0:T(8,128)(2,1)} %param.5), channel_id=1, replica_groups=mesh['z'=8,'xl'=2,'c'=2,'xh'=2,'y'=4] {'z'}, dimensions={0}, use_global_device_ids=true | all-gather | bytes 884736 | tf_op jit(solution)/shard_map/all_gather | solution.py:138
  35.5 1.9 stack.45
  37.4 4.5 %all-to-all-start = ((bf16[8,192,256]{2,1,0:T(8,128)(2,1)}), bf16[8,192,256]{2,1,0:T(8,128)(2,1)S(1)}, u32[]{:S(2)}, u32[]{:S(2)}) async-start(bf16[8,192,256]{2,1,0:T(8,128)(2,1)} %stack.45), calls=%async_computation | async-start | bytes 1572864 | tf_op jit(solution)/shard_map/all_to_all | solution.py:116
  42.3 12.6 %all-to-all-done = bf16[8,192,256]{2,1,0:T(8,128)(2,1)S(1)} async-done(((bf16[8,192,256]{2,1,0:T(8,128)(2,1)}), bf16[8,192,256]{2,1,0:T(8,128)(2,1)S(1)}, u32[]{:S(2)}, u32[]{:S(2)}) %all-to-all-start) | async-done | bytes 786464 | tf_op jit(solution)/shard_map/all_to_all | solution.py:116
  55.0 23.1 %all-gather.2.cloned.1.call-done = bf16[128,48,256]{2,1,0:T(8,128)(2,1)} async-done(((bf16[32,48,256]{2,1,0:T(8,128)(2,1)}), bf16[128,48,256]{2,1,0:T(8,128)(2,1)}) %all-gather.2.cloned.1.call-update) | async-done | bytes 3145744 | tf_op jit(solution)/shard_map/all_gather | solution.py:138
  78.1 60.3 %while.19 = (s32[]{:T(128)}, f32[1536]{0:T(1024)S(1)}, f32[1536]{0:T(1024)S(1)}, f32[1536,256]{1,0:T(8,128)S(1)}, f32[1536]{0:T(1024)S(1)}, /*index=5*/f32[1536]...) while((s32[]{:T(128)}, f32[1536]{0:T(1024)S(1)}, ...), condition=%wide.region_5.6_spmd.clone, body=%wide.region_0.5_spmd.clone.sunk | while | flops 3260167680 | bytes 94312616 | solution.py:102
  78.1 7.6 %multiply_reduce_fusion.5 = (f32[1536]{0:T(1024)S(1)}, f32[2048,1536]{1,0:T(8,128)}) fusion(bf16[1536,256]{1,0:T(8,128)(2,1)S(1)} %get-tuple-element.282, bf16[3,2048,256]{2,1,0:T(8,128)(2,1)} %get-tuple-element.281, s32[]{:T(128)S(6)} %copy.42), kind=kOutput, calls=%fused_computation.3.clone.1 | convolution fusion | flops 1616902656 | bytes 14424068 | tf_op jit(solution)/shard_map/while/body/eval_jaxpr/dot_general | solution.py:81
  85.7 8.4 %multiply_reduce_fusion.6 = (f32[1536]{0:T(1024)S(1)}, f32[1536]{0:T(1024)S(1)}, f32[1536]{0:T(1024)S(1)}) fusion(f32[2048]{0:T(1024)S(1)} %bitcast.91, f32[1536]{0:T(1024)S(1)} %select_maximum_fusion.3, f32[2048,1536]{1,0:T(8,128)} %get-tuple-element.242, f32[2048]{0:T(1024)S(1)} %bitcast.92), kind=kLoop, calls=%fused_computation.clone.1 | loop fusion | flops 22015488 | bytes 12623872 | tf_op jit(solution)/shard_map/while/body/eval_jaxpr/reduce_sum | solution.py:94
  94.2 3.9 %fusion.89 = f32[1536,256]{1,0:T(8,128)S(1)} fusion(f32[1536]{0:T(1024)S(1)} %select_maximum_fusion.3, f32[2048,1536]{1,0:T(8,128)S(1)} %copy-done, f32[1536,256]{1,0:T(8,128)S(1)} %get-tuple-element.266, bf16[3,2048,256]{2,1,0:T(8,128)(2,1)} %get-tuple-element.281, s32[]{:T(128)S(6)} %copy.42, f32[1536]{0:T(1024)S(1)} %get-tuple-element.246, ...), kind=kOutput, calls=%fused_computation.7.clone.1 | convolution fusion | flops 1621229568 | bytes 16789508 | tf_op jit(solution)/shard_map/while/body/eval_jaxpr/dot_general | solution.py:90
  98.2 7.6 %multiply_reduce_fusion.5 = (f32[1536]{0:T(1024)S(1)}, f32[2048,1536]{1,0:T(8,128)}) fusion(bf16[1536,256]{1,0:T(8,128)(2,1)S(1)} %get-tuple-element.282, bf16[3,2048,256]{2,1,0:T(8,128)(2,1)} %get-tuple-element.281, s32[]{:T(128)S(6)} %copy.42), kind=kOutput, calls=%fused_computation.3.clone.1 | convolution fusion | flops 1616902656 | bytes 14424068 | tf_op jit(solution)/shard_map/while/body/eval_jaxpr/dot_general | solution.py:81
  105.8 8.4 %multiply_reduce_fusion.6 = (f32[1536]{0:T(1024)S(1)}, f32[1536]{0:T(1024)S(1)}, f32[1536]{0:T(1024)S(1)}) fusion(f32[2048]{0:T(1024)S(1)} %bitcast.91, f32[1536]{0:T(1024)S(1)} %select_maximum_fusion.3, f32[2048,1536]{1,0:T(8,128)} %get-tuple-element.242, f32[2048]{0:T(1024)S(1)} %bitcast.92), kind=kLoop, calls=%fused_computation.clone.1 | loop fusion | flops 22015488 | bytes 12623872 | tf_op jit(solution)/shard_map/while/body/eval_jaxpr/reduce_sum | solution.py:94
  114.3 3.9 %fusion.89 = f32[1536,256]{1,0:T(8,128)S(1)} fusion(f32[1536]{0:T(1024)S(1)} %select_maximum_fusion.3, f32[2048,1536]{1,0:T(8,128)S(1)} %copy-done, f32[1536,256]{1,0:T(8,128)S(1)} %get-tuple-element.266, bf16[3,2048,256]{2,1,0:T(8,128)(2,1)} %get-tuple-element.281, s32[]{:T(128)S(6)} %copy.42, f32[1536]{0:T(1024)S(1)} %get-tuple-element.246, ...), kind=kOutput, calls=%fused_computation.7.clone.1 | convolution fusion | flops 1621229568 | bytes 16789508 | tf_op jit(solution)/shard_map/while/body/eval_jaxpr/dot_general | solution.py:90
  118.3 7.6 %multiply_reduce_fusion.5 = (f32[1536]{0:T(1024)S(1)}, f32[2048,1536]{1,0:T(8,128)}) fusion(bf16[1536,256]{1,0:T(8,128)(2,1)S(1)} %get-tuple-element.282, bf16[3,2048,256]{2,1,0:T(8,128)(2,1)} %get-tuple-element.281, s32[]{:T(128)S(6)} %copy.42), kind=kOutput, calls=%fused_computation.3.clone.1 | convolution fusion | flops 1616902656 | bytes 14424068 | tf_op jit(solution)/shard_map/while/body/eval_jaxpr/dot_general | solution.py:81
  125.9 8.4 %multiply_reduce_fusion.6 = (f32[1536]{0:T(1024)S(1)}, f32[1536]{0:T(1024)S(1)}, f32[1536]{0:T(1024)S(1)}) fusion(f32[2048]{0:T(1024)S(1)} %bitcast.91, f32[1536]{0:T(1024)S(1)} %select_maximum_fusion.3, f32[2048,1536]{1,0:T(8,128)} %get-tuple-element.242, f32[2048]{0:T(1024)S(1)} %bitcast.92), kind=kLoop, calls=%fused_computation.clone.1 | loop fusion | flops 22015488 | bytes 12623872 | tf_op jit(solution)/shard_map/while/body/eval_jaxpr/reduce_sum | solution.py:94
  134.4 3.9 %fusion.89 = f32[1536,256]{1,0:T(8,128)S(1)} fusion(f32[1536]{0:T(1024)S(1)} %select_maximum_fusion.3, f32[2048,1536]{1,0:T(8,128)S(1)} %copy-done, f32[1536,256]{1,0:T(8,128)S(1)} %get-tuple-element.266, bf16[3,2048,256]{2,1,0:T(8,128)(2,1)} %get-tuple-element.281, s32[]{:T(128)S(6)} %copy.42, f32[1536]{0:T(1024)S(1)} %get-tuple-element.246, ...), kind=kOutput, calls=%fused_computation.7.clone.1 | convolution fusion | flops 1621229568 | bytes 16789508 | tf_op jit(solution)/shard_map/while/body/eval_jaxpr/dot_general | solution.py:90
  140.1 4.4 %all-to-all-start.1 = ((f32[8,196,256]{2,1,0:T(8,128)}), f32[8,196,256]{2,1,0:T(8,128)S(1)}, u32[]{:S(2)}, u32[]{:S(2)}) async-start(f32[8,196,256]{2,1,0:T(8,128)} %select_maximum_fusion.1), calls=%async_computation.1 | async-start | bytes 3276800 | tf_op jit(solution)/shard_map/all_to_all | solution.py:168
  144.6 22.2 %all-to-all-done.1 = f32[8,196,256]{2,1,0:T(8,128)S(1)} async-done(((f32[8,196,256]{2,1,0:T(8,128)}), f32[8,196,256]{2,1,0:T(8,128)S(1)}, u32[]{:S(2)}, u32[]{:S(2)}) %all-to-all-start.1) | async-done | bytes 1605664 | tf_op jit(solution)/shard_map/all_to_all | solution.py:168
  167.2 1.9 collective-permute-start.4
  169.1 2.4 %collective-permute-start.5 = (f32[2,1,48]{2,1,0:T(1,128)S(1)}, f32[2,1,48]{2,1,0:T(1,128)S(1)}, u32[]{:S(2)}, u32[]{:S(2)}) collective-permute-start(f32[2,1,48]{2,1,0:T(1,128)S(1)} %get-tuple-element.162), channel_id=1, source_target_pairs={{0,8},{8,16},{16,24},{24,32},{32,40},{40,48},{48,56},{56,64},{64,7... | collective-permute-start | bytes 1160 | tf_op jit(solution)/shard_map/ppermute | solution.py:25
  172.5 5.3 %collective-permute-start.1 = (bf16[2,1,48,256]{3,2,1,0:T(8,128)(2,1)S(1)}, bf16[2,1,48,256]{3,2,1,0:T(8,128)(2,1)S(1)}, u32[]{:S(2)}, u32[]{:S(2)}) collective-permute-start(bf16[2,1,48,256]{3,2,1,0:T(8,128)(2,1)S(1)} %get-tuple-element.159), channel_id=1, source_target_pairs={{8,0},{16,8},{24,16},{32,24},{40,32},{48,40},{56,48},{64,56},{72,6... | collective-permute-start | bytes 147464 | tf_op jit(solution)/shard_map/ppermute | solution.py:26
  177.8 1.9 collective-permute-start
  179.8 5.5 %collective-permute-done = bf16[2,1,48,256]{3,2,1,0:T(8,128)(2,1)S(1)} collective-permute-done((bf16[2,1,48,256]{3,2,1,0:T(8,128)(2,1)S(1)}, bf16[2,1,48,256]{3,2,1,0:T(8,128)(2,1)S(1)}, u32[]{:S(2)}, u32[]{:S(2)}) %collective-permute-start) | collective-permute-done | bytes 49184 | tf_op jit(solution)/shard_map/ppermute | solution.py:25
  185.3 4.1 %collective-permute-start.3 = (bf16[2,6,1,256]{3,2,1,0:T(2,128)(2,1)S(1)}, bf16[2,6,1,256]{3,2,1,0:T(2,128)(2,1)S(1)}, u32[]{:S(2)}, u32[]{:S(2)}) collective-permute-start(bf16[2,6,1,256]{3,2,1,0:T(2,128)(2,1)S(1)} %get-tuple-element.157), channel_id=1, source_target_pairs={{1,0},{2,1},{3,2},{4,3},{5,4},{6,5},{7,6},{9,8},{10,9},{11,10},{12... | collective-permute-start | bytes 18440 | tf_op jit(solution)/shard_map/ppermute | solution.py:26
  189.5 1.9 collective-permute-start.2
  191.5 2.3 collective-permute-start.7
  193.7 7.2 %collective-permute-start.6 = (f32[2,6,1]{2,1,0:T(8,128)S(1)}, f32[2,6,1]{2,1,0:T(8,128)S(1)}, u32[]{:S(2)}, u32[]{:S(2)}) collective-permute-start(f32[2,6,1]{2,1,0:T(8,128)S(1)} %get-tuple-element.160), channel_id=1, source_target_pairs={{1,0},{2,1},{3,2},{4,3},{5,4},{6,5},{7,6},{9,8},{10,9},{11,10},{12... | collective-permute-start | bytes 152 | tf_op jit(solution)/shard_map/ppermute | solution.py:26
  202.4 1.9 collective-permute-start.9
  204.4 2.4 %collective-permute-start.8 = (bf16[3,1,48,256]{3,2,1,0:T(8,128)(2,1)S(1)}, bf16[3,1,48,256]{3,2,1,0:T(8,128)(2,1)S(1)}, u32[]{:S(2)}, u32[]{:S(2)}) collective-permute-start(bf16[3,1,48,256]{3,2,1,0:T(8,128)(2,1)S(1)} %get-tuple-element.154), channel_id=1, source_target_pairs={{0,8},{8,16},{16,24},{24,32},{32,40},{40,48},{48,56},{56,64},{64,7... | collective-permute-start | bytes 221192 | tf_op jit(solution)/shard_map/ppermute | solution.py:25
  207.0 5.2 %collective-permute-done.8 = bf16[3,1,48,256]{3,2,1,0:T(8,128)(2,1)S(1)} collective-permute-done((bf16[3,1,48,256]{3,2,1,0:T(8,128)(2,1)S(1)}, bf16[3,1,48,256]{3,2,1,0:T(8,128)(2,1)S(1)}, u32[]{:S(2)}, u32[]{:S(2)}) %collective-permute-start.8) | collective-permute-done | bytes 73760 | tf_op jit(solution)/shard_map/ppermute | solution.py:25
  212.2 3.9 %collective-permute-start.11 = (bf16[3,6,1,256]{3,2,1,0:T(2,128)(2,1)S(1)}, bf16[3,6,1,256]{3,2,1,0:T(2,128)(2,1)S(1)}, u32[]{:S(2)}, u32[]{:S(2)}) collective-permute-start(bf16[3,6,1,256]{3,2,1,0:T(2,128)(2,1)S(1)} %get-tuple-element.148), channel_id=1, source_target_pairs={{1,0},{2,1},{3,2},{4,3},{5,4},{6,5},{7,6},{9,8},{10,9},{11,10},{12... | collective-permute-start | bytes 27656 | tf_op jit(solution)/shard_map/ppermute | solution.py:26
  216.1 1.9 collective-permute-start.10
  218.7 6.7 %collective-permute-done.10 = bf16[3,6,1,256]{3,2,1,0:T(2,128)(2,1)S(1)} collective-permute-done((bf16[3,6,1,256]{3,2,1,0:T(2,128)(2,1)S(1)}, bf16[3,6,1,256]{3,2,1,0:T(2,128)(2,1)S(1)}, u32[]{:S(2)}, u32[]{:S(2)}) %collective-permute-start.10) | collective-permute-done | bytes 9248 | tf_op jit(solution)/shard_map/ppermute | solution.py:25
  (87 shorter events, 7.5 us)
Async XLA Ops:
  7.2 70.9 %all-gather.2.cloned.1.call-start = ((), (), s32[]{:S(2)}) async-start(), calls=%async_computation.2 | async-start | bytes 3932160 | tf_op jit(solution)/shard_map/all_gather | solution.py:138
  37.4 17.6 %all-to-all-start = ((bf16[8,192,256]{2,1,0:T(8,128)(2,1)}), bf16[8,192,256]{2,1,0:T(8,128)(2,1)S(1)}, u32[]{:S(2)}, u32[]{:S(2)}) async-start(bf16[8,192,256]{2,1,0:T(8,128)(2,1)} %stack.45), calls=%async_computation | async-start | bytes 1572864 | tf_op jit(solution)/shard_map/all_to_all | solution.py:116
  85.7 8.5 %copy-start = (f32[2048,1536]{1,0:T(8,128)S(1)}, f32[2048,1536]{1,0:T(8,128)}, u32[]{:S(2)}) copy-start(f32[2048,1536]{1,0:T(8,128)} %get-tuple-element.242) | copy-start | bytes 37748740 | tf_op jit(solution)/shard_map/while
  105.8 8.5 %copy-start = (f32[2048,1536]{1,0:T(8,128)S(1)}, f32[2048,1536]{1,0:T(8,128)}, u32[]{:S(2)}) copy-start(f32[2048,1536]{1,0:T(8,128)} %get-tuple-element.242) | copy-start | bytes 37748740 | tf_op jit(solution)/shard_map/while
  125.9 8.5 %copy-start = (f32[2048,1536]{1,0:T(8,128)S(1)}, f32[2048,1536]{1,0:T(8,128)}, u32[]{:S(2)}) copy-start(f32[2048,1536]{1,0:T(8,128)} %get-tuple-element.242) | copy-start | bytes 37748740 | tf_op jit(solution)/shard_map/while
  140.1 31.8 %copy-start.1 = (bf16[4,48,256]{2,1,0:T(8,128)(2,1)S(1)}, bf16[4,48,256]{2,1,0:T(8,128)(2,1)}, u32[]{:S(2)}) copy-start(bf16[4,48,256]{2,1,0:T(8,128)(2,1)} %param.4) | copy-start | bytes 294916
  140.1 26.7 %all-to-all-start.1 = ((f32[8,196,256]{2,1,0:T(8,128)}), f32[8,196,256]{2,1,0:T(8,128)S(1)}, u32[]{:S(2)}, u32[]{:S(2)}) async-start(f32[8,196,256]{2,1,0:T(8,128)} %select_maximum_fusion.1), calls=%async_computation.1 | async-start | bytes 3276800 | tf_op jit(solution)/shard_map/all_to_all | solution.py:168
  167.2 12.5 %collective-permute-start.4 = (f32[2,1,48]{2,1,0:T(1,128)S(1)}, f32[2,1,48]{2,1,0:T(1,128)S(1)}, u32[]{:S(2)}, u32[]{:S(2)}) collective-permute-start(f32[2,1,48]{2,1,0:T(1,128)S(1)} %get-tuple-element.163), channel_id=1, source_target_pairs={{8,0},{16,8},{24,16},{32,24},{40,32},{48,40},{56,48},{64,56},{72,6... | collective-permute-start | bytes 1160 | tf_op jit(solution)/shard_map/ppermute | solution.py:26
  169.1 10.6 %collective-permute-start.5 = (f32[2,1,48]{2,1,0:T(1,128)S(1)}, f32[2,1,48]{2,1,0:T(1,128)S(1)}, u32[]{:S(2)}, u32[]{:S(2)}) collective-permute-start(f32[2,1,48]{2,1,0:T(1,128)S(1)} %get-tuple-element.162), channel_id=1, source_target_pairs={{0,8},{8,16},{16,24},{24,32},{32,40},{40,48},{48,56},{56,64},{64,7... | collective-permute-start | bytes 1160 | tf_op jit(solution)/shard_map/ppermute | solution.py:25
  172.5 7.2 %collective-permute-start.1 = (bf16[2,1,48,256]{3,2,1,0:T(8,128)(2,1)S(1)}, bf16[2,1,48,256]{3,2,1,0:T(8,128)(2,1)S(1)}, u32[]{:S(2)}, u32[]{:S(2)}) collective-permute-start(bf16[2,1,48,256]{3,2,1,0:T(8,128)(2,1)S(1)} %get-tuple-element.159), channel_id=1, source_target_pairs={{8,0},{16,8},{24,16},{32,24},{40,32},{48,40},{56,48},{64,56},{72,6... | collective-permute-start | bytes 147464 | tf_op jit(solution)/shard_map/ppermute | solution.py:26
  177.8 7.5 %collective-permute-start = (bf16[2,1,48,256]{3,2,1,0:T(8,128)(2,1)S(1)}, bf16[2,1,48,256]{3,2,1,0:T(8,128)(2,1)S(1)}, u32[]{:S(2)}, u32[]{:S(2)}) collective-permute-start(bf16[2,1,48,256]{3,2,1,0:T(8,128)(2,1)S(1)} %get-tuple-element.158), channel_id=1, source_target_pairs={{0,8},{8,16},{16,24},{24,32},{32,40},{40,48},{48,56},{56,64},{64,7... | collective-permute-start | bytes 147464 | tf_op jit(solution)/shard_map/ppermute | solution.py:25
  185.3 15.6 %collective-permute-start.3 = (bf16[2,6,1,256]{3,2,1,0:T(2,128)(2,1)S(1)}, bf16[2,6,1,256]{3,2,1,0:T(2,128)(2,1)S(1)}, u32[]{:S(2)}, u32[]{:S(2)}) collective-permute-start(bf16[2,6,1,256]{3,2,1,0:T(2,128)(2,1)S(1)} %get-tuple-element.157), channel_id=1, source_target_pairs={{1,0},{2,1},{3,2},{4,3},{5,4},{6,5},{7,6},{9,8},{10,9},{11,10},{12... | collective-permute-start | bytes 18440 | tf_op jit(solution)/shard_map/ppermute | solution.py:26
  189.5 11.5 %collective-permute-start.2 = (bf16[2,6,1,256]{3,2,1,0:T(2,128)(2,1)S(1)}, bf16[2,6,1,256]{3,2,1,0:T(2,128)(2,1)S(1)}, u32[]{:S(2)}, u32[]{:S(2)}) collective-permute-start(bf16[2,6,1,256]{3,2,1,0:T(2,128)(2,1)S(1)} %get-tuple-element.156), channel_id=1, source_target_pairs={{0,1},{1,2},{2,3},{3,4},{4,5},{5,6},{6,7},{8,9},{9,10},{10,11},{11... | collective-permute-start | bytes 18440 | tf_op jit(solution)/shard_map/ppermute | solution.py:25
  191.5 15.4 %collective-permute-start.7 = (f32[2,6,1]{2,1,0:T(8,128)S(1)}, f32[2,6,1]{2,1,0:T(8,128)S(1)}, u32[]{:S(2)}, u32[]{:S(2)}) collective-permute-start(f32[2,6,1]{2,1,0:T(8,128)S(1)} %get-tuple-element.161), channel_id=1, source_target_pairs={{0,1},{1,2},{2,3},{3,4},{4,5},{5,6},{6,7},{8,9},{9,10},{10,11},{11... | collective-permute-start | bytes 152 | tf_op jit(solution)/shard_map/ppermute | solution.py:25
  193.7 13.1 %collective-permute-start.6 = (f32[2,6,1]{2,1,0:T(8,128)S(1)}, f32[2,6,1]{2,1,0:T(8,128)S(1)}, u32[]{:S(2)}, u32[]{:S(2)}) collective-permute-start(f32[2,6,1]{2,1,0:T(8,128)S(1)} %get-tuple-element.160), channel_id=1, source_target_pairs={{1,0},{2,1},{3,2},{4,3},{5,4},{6,5},{7,6},{9,8},{10,9},{11,10},{12... | collective-permute-start | bytes 152 | tf_op jit(solution)/shard_map/ppermute | solution.py:26
  202.4 4.5 %collective-permute-start.9 = (bf16[3,1,48,256]{3,2,1,0:T(8,128)(2,1)S(1)}, bf16[3,1,48,256]{3,2,1,0:T(8,128)(2,1)S(1)}, u32[]{:S(2)}, u32[]{:S(2)}) collective-permute-start(bf16[3,1,48,256]{3,2,1,0:T(8,128)(2,1)S(1)} %get-tuple-element.155), channel_id=1, source_target_pairs={{8,0},{16,8},{24,16},{32,24},{40,32},{48,40},{56,48},{64,56},{72,6... | collective-permute-start | bytes 221192 | tf_op jit(solution)/shard_map/ppermute | solution.py:26
  204.4 7.8 %collective-permute-start.8 = (bf16[3,1,48,256]{3,2,1,0:T(8,128)(2,1)S(1)}, bf16[3,1,48,256]{3,2,1,0:T(8,128)(2,1)S(1)}, u32[]{:S(2)}, u32[]{:S(2)}) collective-permute-start(bf16[3,1,48,256]{3,2,1,0:T(8,128)(2,1)S(1)} %get-tuple-element.154), channel_id=1, source_target_pairs={{0,8},{8,16},{16,24},{24,32},{32,40},{40,48},{48,56},{56,64},{64,7... | collective-permute-start | bytes 221192 | tf_op jit(solution)/shard_map/ppermute | solution.py:25
  212.2 6.5 %collective-permute-start.11 = (bf16[3,6,1,256]{3,2,1,0:T(2,128)(2,1)S(1)}, bf16[3,6,1,256]{3,2,1,0:T(2,128)(2,1)S(1)}, u32[]{:S(2)}, u32[]{:S(2)}) collective-permute-start(bf16[3,6,1,256]{3,2,1,0:T(2,128)(2,1)S(1)} %get-tuple-element.148), channel_id=1, source_target_pairs={{1,0},{2,1},{3,2},{4,3},{5,4},{6,5},{7,6},{9,8},{10,9},{11,10},{12... | collective-permute-start | bytes 27656 | tf_op jit(solution)/shard_map/ppermute | solution.py:26
  216.1 9.3 %collective-permute-start.10 = (bf16[3,6,1,256]{3,2,1,0:T(2,128)(2,1)S(1)}, bf16[3,6,1,256]{3,2,1,0:T(2,128)(2,1)S(1)}, u32[]{:S(2)}, u32[]{:S(2)}) collective-permute-start(bf16[3,6,1,256]{3,2,1,0:T(2,128)(2,1)S(1)} %get-tuple-element.147), channel_id=1, source_target_pairs={{0,1},{1,2},{2,3},{3,4},{4,5},{5,6},{6,7},{8,9},{9,10},{10,11},{11... | collective-permute-start | bytes 27656 | tf_op jit(solution)/shard_map/ppermute | solution.py:25
Sparse Core Ops, SparseCore 0:
  35.6 42.4 all-gather.1
